TPU v7x, 512 devices: a whole 4x8x8 slice. The times are simulated.
512 devices in a mesh: area: 128 (over z, y, core), blk: 4 (over x).
Axes of the slice: x: 4, y: 8, z: 8, core: 2. Of those that a mesh axis runs over, the one named last changes fastest.
Arguments:
- activity: float32 [1024, 4, 64, 128], P('area', 'blk'), may hold values from -8 to 8
- ext_input: bfloat16 [1024, 4, 64, 128], P('area', 'blk'), may hold values from -5 to 5
- weights: bfloat16 [384, 4, 128, 512], P('area', 'blk'), may hold values from -0.25 to 0.25
- slot_dst: int32 [384], P('area'), may hold values from 0 to 7
- slot_src: int32 [384], P('area'), may hold values from 0 to 1023, as said below
- slot_count: int32 [128], P('area'), may hold values from 3 to 3, as said below
- hebb_mask: int32 [384], P('area'), may hold values 0 or 1
Outputs:
- final_activity: float32 [1024, 4, 64, 128], P('area', 'blk')
- plasticity: bfloat16 [384, 4, 128, 512], P('area', 'blk')
Inputs may be any that keep to these rules, and one draw needn't show every extreme that they name: Index i of area holds area i // 4; sources lie in areas listed for it by a connectome over the areas that always lists the area itself, the areas beside it on both sides (counted round) and the opposite one. Slots 0, 1 and 2 of index i of area have their source sub-blocks held by indices (i - 1) mod 128, (i + 1) mod 128 and (i + 64) mod 128. Among the occupied slots of one index of area, at most 1 have source sub-blocks held by one index of area (slot_src // 8); some index of area reaches 1. `slot_count`: some index of area has all 3 slots occupied.
All inputs are finite; a program needn't handle non-finite values. No bound on the sum of `hebb_mask` on one device may be relied on, other than what follows from the above.
Results may differ from a plain program's by a relative error of at most 0.014.
Values may be sent and summed in bfloat16 or wider, within the bound.
No kernel may reach another device: no remote copies, remote signals or barrier semaphores. Data moves between devices by JAX's collectives and lax.ppermute only.
A program may use at most 64 MiB of HBM per device.

v0:
```python
import jax
import jax.numpy as jnp
from jax import lax
from jax.sharding import PartitionSpec as P

STEPS = 4
euler_step = 0.5


def request_rosters(src_rows, count_now, sub_dev, n_areas, link_cap):
    slot_cap = src_rows.shape[0]
    slot_ids = jnp.arange(slot_cap)
    occupied = slot_ids < count_now
    owner_idx = src_rows // sub_dev
    local_idx = src_rows % sub_dev
    earlier = (
        (owner_idx[:, None] == owner_idx[None, :])
        & occupied[None, :]
        & (slot_ids[None, :] < slot_ids[:, None])
    )
    link_idx = jnp.minimum(jnp.sum(earlier.astype(jnp.int32), axis=1), link_cap - 1)
    matches = (
        occupied[:, None, None]
        & (owner_idx[:, None, None] == jnp.arange(n_areas)[None, :, None])
        & (link_idx[:, None, None] == jnp.arange(link_cap)[None, None, :])
    )
    request_table = jnp.sum(jnp.where(matches, (local_idx + 1)[:, None, None], 0), axis=0)
    return (occupied, owner_idx, link_idx, request_table)


def body(activity, ext_input, weights, slot_dst, slot_src, slot_count, hebb_mask):
    n_areas = lax.axis_size("area")
    my_blk = lax.axis_index("blk")
    sub_dev = activity.shape[0]
    trials = activity.shape[2]
    quarter = activity.shape[3]
    slot_cap = slot_src.shape[0]
    sub_width = weights.shape[3]
    link_cap = (slot_cap + n_areas - 1) // n_areas
    occupied, owner_idx, link_idx, request_table = request_rosters(
        slot_src, slot_count[0], sub_dev, n_areas, link_cap
    )
    needed_rows = lax.all_to_all(request_table, "area", split_axis=0, concat_axis=0, tiled=True)
    is_valid = needed_rows > 0
    pick_idx = jnp.maximum(needed_rows - 1, 0)
    select = ((slot_dst[:, None] == jnp.arange(sub_dev)[None, :]) & occupied[:, None]).astype(
        jnp.float32
    )
    slot_weights = weights[:, 0]
    pre_list = []
    post_list = []
    full_act, full_ext = (
        lax.all_gather(activity.astype(jnp.bfloat16), "blk", axis=1, tiled=True).astype(
            activity.dtype
        ),
        lax.all_gather(
            ext_input.astype(jnp.float32).astype(jnp.bfloat16), "blk", axis=1, tiled=True
        ).astype(jnp.float32),
    )
    current = full_act.transpose(0, 2, 1, 3).reshape(sub_dev, trials, sub_width)
    drive_in = full_ext.transpose(0, 2, 1, 3).reshape(sub_dev, trials, sub_width)
    rate_full = jnp.tanh(current).astype(jnp.bfloat16)
    for step_idx in range(STEPS):
        rates_own = lax.dynamic_slice_in_dim(rate_full, my_blk * quarter, quarter, 2)
        outbound_rates = jnp.where(
            is_valid[:, :, None, None], rates_own[pick_idx], jnp.zeros((), jnp.bfloat16)
        )
        presynaptic_rates = lax.all_to_all(
            outbound_rates, "area", split_axis=0, concat_axis=0, tiled=True
        )[owner_idx, link_idx]
        input_contribution = jnp.einsum(
            "xvy,xye->xve", presynaptic_rates, slot_weights, preferred_element_type=jnp.float32
        )
        partial_value = jnp.einsum(
            "kd,kts->dts", select, input_contribution, precision=lax.Precision.HIGHEST
        )
        partial_value, presynaptic_rates = (partial_value, presynaptic_rates)
        summed = lax.psum(partial_value.astype(jnp.bfloat16), "blk").astype(jnp.float32)
        current = current + euler_step * (summed - current + drive_in)
        rate_full = jnp.tanh(current).astype(jnp.bfloat16)
        pre_list.append(presynaptic_rates)
        post_list.append(rate_full)
    final_state = lax.dynamic_slice_in_dim(current, my_blk * quarter, quarter, 2)[:, None]
    pre_all = jnp.stack(pre_list, axis=1).astype(jnp.float32)
    pre_centered = (pre_all - jnp.mean(pre_all, axis=2, keepdims=True)).astype(jnp.bfloat16)
    pre_centered = pre_centered.reshape(slot_cap, STEPS * trials, quarter)
    post_all = jnp.stack(post_list, axis=1).astype(jnp.float32)
    post_centered = (post_all - jnp.mean(post_all, axis=2, keepdims=True)).astype(jnp.bfloat16)
    post_slot = post_centered[slot_dst].reshape(slot_cap, STEPS * trials, sub_width)
    change = jnp.einsum("knq,kns->kqs", pre_centered, post_slot, preferred_element_type=jnp.float32)
    gate_on = (occupied & (hebb_mask == 1)).astype(jnp.float32)
    norm_scale = (STEPS * trials) ** (-0.5)
    plasticity = (change * gate_on[:, None, None] * norm_scale).astype(jnp.bfloat16)[:, None]
    return (final_state, plasticity)


def solution(mesh):
    in_specs = (
        P("area", "blk", None, None),
        P("area", "blk", None, None),
        P("area", "blk", None, None),
        P("area"),
        P("area"),
        P("area"),
        P("area"),
    )
    out_specs = (P("area", "blk", None, None), P("area", "blk", None, None))
    return jax.shard_map(body, mesh=mesh, in_specs=in_specs, out_specs=out_specs, check_vma=False)
```

profile of v0, /device:TPU:8, one launch (start us, length us, event | category | flops | bytes accessed | tf_op | source)
XLA Modules:
  0.0 565.2 jit_solution(8893313728588876898)
XLA Ops:
  11.3 17.4 %all-to-all-start = ((s32[128,1,1]{2,1,0:T(1,128)}), s32[128,1,1]{2,1,0:T(1,128)S(1)}, u32[]{:S(2)}, u32[]{:S(2)}) async-start(s32[128,1,1]{2,1,0:T(1,128)} %copy.91), calls=%async_computation | async-start | bytes 131072 | tf_op jit(solution)/shard_map/all_to_all | solution.py:43
  29.7 13.1 %all_gather.6 = bf16[8,4,64,128]{3,2,1,0:T(8,128)(2,1)S(1)} all-gather(bf16[8,1,64,128]{3,2,1,0:T(8,128)(2,1)S(1)} %convert_element_type.74), channel_id=1, replica_groups=mesh['area'=128,'blk'=4] {'blk'}, dimensions={1}, use_global_device_ids=true | all-gather | bytes 655360 | tf_op jit(solution)/shard_map/all_gather | solution.py:53
  43.7 2.4 maximum_reduce_fusion
  46.0 2.2 gather_fusion
  48.2 2.4 compare_reduce_fusion
  50.6 3.2 fusion.4
  53.7 13.7 %all-to-all-start.1 = ((bf16[128,1,64,128]{3,2,1,0:T(8,128)(2,1)}), bf16[128,1,64,128]{3,2,1,0:T(8,128)(2,1)S(1)}, u32[]{:S(2)}, u32[]{:S(2)}) async-start(bf16[128,1,64,128]{3,2,1,0:T(8,128)(2,1)} %fusion.4), calls=%async_computation.1 | async-start | bytes 4194304 | tf_op jit(solution)/shard_map/all_to_all | solution.py:68
  68.9 52.5 %all-to-all-done.1 = bf16[128,1,64,128]{3,2,1,0:T(8,128)(2,1)S(1)} async-done(((bf16[128,1,64,128]{3,2,1,0:T(8,128)(2,1)}), bf16[128,1,64,128]{3,2,1,0:T(8,128)(2,1)S(1)}, u32[]{:S(2)}, u32[]{:S(2)}) %all-to-all-start.1) | async-done | bytes 2097184 | tf_op jit(solution)/shard_map/all_to_all | solution.py:68
  125.5 14.4 %all_gather.7 = bf16[8,4,64,128]{3,2,1,0:T(8,128)(2,1)S(1)} all-gather(bf16[8,1,64,128]{3,2,1,0:T(8,128)(2,1)S(1)} %copy-done.10), channel_id=1, replica_groups=mesh['area'=128,'blk'=4] {'blk'}, dimensions={1}, use_global_device_ids=true | all-gather | bytes 655360 | tf_op jit(solution)/shard_map/all_gather | solution.py:56
  140.0 32.7 %all-reduce.5.cloned.1.call-done = bf16[8,64,512]{2,0,1:T(8,128)(2,1)} async-done(((bf16[8,64,512]{2,0,1:T(8,128)(2,1)}), bf16[8,64,512]{2,0,1:T(8,128)(2,1)}) %all-reduce.5.cloned.1.call-update) | async-done | bytes 524304 | tf_op jit(solution)/shard_map/psum | solution.py:78
  172.6 2.2 tanh_convert_fusion.3
  175.7 2.2 gather_fusion.2
  179.7 68.1 %all_to_all.29 = bf16[128,1,64,128]{3,2,1,0:T(8,128)(2,1)} all-to-all(bf16[128,1,64,128]{3,2,1,0:T(8,128)(2,1)S(1)} %fusion.3), channel_id=1, replica_groups=mesh['area'=128,'blk'=4] {'area'}, dimensions={0} | all-to-all | bytes 4194304 | tf_op jit(solution)/shard_map/all_to_all | solution.py:68
  247.8 2.2 gather_fusion.3
  252.0 46.3 %all-reduce.7.cloned.1.call-done = bf16[8,64,512]{2,0,1:T(8,128)(2,1)} async-done(((bf16[8,64,512]{2,0,1:T(8,128)(2,1)}), bf16[8,64,512]{2,0,1:T(8,128)(2,1)}) %all-reduce.7.cloned.1.call-update) | async-done | bytes 524304 | tf_op jit(solution)/shard_map/psum | solution.py:78
  298.3 2.3 tanh_convert_fusion.2
  305.4 68.1 %all_to_all.30 = bf16[128,1,64,128]{3,2,1,0:T(8,128)(2,1)} all-to-all(bf16[128,1,64,128]{3,2,1,0:T(8,128)(2,1)S(1)} %fusion.2), channel_id=1, replica_groups=mesh['area'=128,'blk'=4] {'area'}, dimensions={0} | all-to-all | bytes 4194304 | tf_op jit(solution)/shard_map/all_to_all | solution.py:68
  377.5 46.4 %all-reduce.9.cloned.1.call-done = bf16[8,64,512]{2,0,1:T(8,128)(2,1)} async-done(((bf16[8,64,512]{2,0,1:T(8,128)(2,1)}), bf16[8,64,512]{2,0,1:T(8,128)(2,1)}) %all-reduce.9.cloned.1.call-update) | async-done | bytes 524304 | tf_op jit(solution)/shard_map/psum | solution.py:78
  423.9 2.6 tanh_convert_fusion.1
  429.5 3.1 fusion.1
  432.6 15.0 %all-to-all-start.4 = ((bf16[128,1,64,128]{3,2,1,0:T(8,128)(2,1)}), bf16[128,1,64,128]{3,2,1,0:T(8,128)(2,1)}, u32[]{:S(2)}, u32[]{:S(2)}) async-start(bf16[128,1,64,128]{3,2,1,0:T(8,128)(2,1)} %fusion.1), calls=%async_computation.4 | async-start | bytes 4194304 | tf_op jit(solution)/shard_map/all_to_all | solution.py:68
  447.7 53.6 %all-to-all-done.4 = bf16[128,1,64,128]{3,2,1,0:T(8,128)(2,1)} async-done(((bf16[128,1,64,128]{3,2,1,0:T(8,128)(2,1)}), bf16[128,1,64,128]{3,2,1,0:T(8,128)(2,1)}, u32[]{:S(2)}, u32[]{:S(2)}) %all-to-all-start.4) | async-done | bytes 2097184 | tf_op jit(solution)/shard_map/all_to_all | solution.py:68
  506.1 45.5 %all-reduce.11.cloned.1.call-done = bf16[8,64,512]{2,0,1:T(8,128)(2,1)} async-done(((bf16[8,64,512]{2,0,1:T(8,128)(2,1)}), bf16[8,64,512]{2,0,1:T(8,128)(2,1)}) %all-reduce.11.cloned.1.call-update) | async-done | bytes 524304 | tf_op jit(solution)/shard_map/psum | solution.py:78
  551.7 3.0 fusion.16
  (89 shorter events, 36.0 us)
Async XLA Ops:
  7.2 115.5 %copy-start = (bf16[3,1,128,512]{3,2,1,0:T(8,128)(2,1)S(1)}, bf16[3,1,128,512]{3,2,1,0:T(8,128)(2,1)}, u32[]{:S(2)}) copy-start(bf16[3,1,128,512]{3,2,1,0:T(8,128)(2,1)} %param.9) | copy-start | bytes 1179652
  9.7 19.0 %copy-start.11 = (pred[3]{0:T(512)(128)(4,1)}, pred[3]{0:T(512)(128)(4,1)S(1)}, u32[]{:S(2)}) copy-start(pred[3]{0:T(512)(128)(4,1)S(1)} %get-tuple-element.19) | copy-start | bytes 13
  9.9 0.6 copy-start.13
  11.3 32.3 %all-to-all-start = ((s32[128,1,1]{2,1,0:T(1,128)}), s32[128,1,1]{2,1,0:T(1,128)S(1)}, u32[]{:S(2)}, u32[]{:S(2)}) async-start(s32[128,1,1]{2,1,0:T(1,128)} %copy.91), calls=%async_computation | async-start | bytes 131072 | tf_op jit(solution)/shard_map/all_to_all | solution.py:43
  53.7 67.8 %all-to-all-start.1 = ((bf16[128,1,64,128]{3,2,1,0:T(8,128)(2,1)}), bf16[128,1,64,128]{3,2,1,0:T(8,128)(2,1)S(1)}, u32[]{:S(2)}, u32[]{:S(2)}) async-start(bf16[128,1,64,128]{3,2,1,0:T(8,128)(2,1)} %fusion.4), calls=%async_computation.1 | async-start | bytes 4194304 | tf_op jit(solution)/shard_map/all_to_all | solution.py:68
  67.5 105.2 %all-reduce.5.cloned.1.call-start = ((), (), s32[]{:S(2)}) async-start(), calls=%async_computation.5 | async-start | bytes 1048576 | tf_op jit(solution)/shard_map/psum | solution.py:78
  122.7 2.8 copy-start.10
  125.4 172.9 %all-reduce.7.cloned.1.call-start = ((), (), s32[]{:S(2)}) async-start(), calls=%async_computation.6 | async-start | bytes 1048576 | tf_op jit(solution)/shard_map/psum | solution.py:78
  174.9 0.8 copy-start.4
  247.8 50.5 %copy-start.1 = (bf16[8,64,512]{2,0,1:T(8,128)(2,1)S(1)}, bf16[8,64,512]{2,0,1:T(8,128)(2,1)}, u32[]{:S(2)}) copy-start(bf16[8,64,512]{2,0,1:T(8,128)(2,1)} %all-reduce.5.cloned.1.call-done) | copy-start | bytes 1572868
  251.9 172.0 %all-reduce.9.cloned.1.call-start = ((), (), s32[]{:S(2)}) async-start(), calls=%async_computation.7 | async-start | bytes 1048576 | tf_op jit(solution)/shard_map/psum | solution.py:78
  300.6 0.8 copy-start.2
  426.5 0.8 copy-start.6
  432.6 15.0 %copy-start.14 = (s32[3]{0:T(128)S(1)}, s32[3]{0:T(128)}, u32[]{:S(2)}) copy-start(s32[3]{0:T(128)} %param.10) | copy-start | bytes 40
  432.6 68.6 %all-to-all-start.4 = ((bf16[128,1,64,128]{3,2,1,0:T(8,128)(2,1)}), bf16[128,1,64,128]{3,2,1,0:T(8,128)(2,1)}, u32[]{:S(2)}, u32[]{:S(2)}) async-start(bf16[128,1,64,128]{3,2,1,0:T(8,128)(2,1)} %fusion.1), calls=%async_computation.4 | async-start | bytes 4194304 | tf_op jit(solution)/shard_map/all_to_all | solution.py:68
  447.6 57.7 %copy-start.9 = (bf16[3,64,128]{2,1,0:T(8,128)(2,1)S(1)}, bf16[3,64,128]{2,1,0:T(8,128)(2,1)}, u32[]{:S(2)}) copy-start(bf16[3,64,128]{2,1,0:T(8,128)(2,1)} %gather_fusion.1) | copy-start | bytes 147460
  447.6 104.1 %all-reduce.11.cloned.1.call-start = ((), (), s32[]{:S(2)}) async-start(), calls=%async_computation.8 | async-start | bytes 1048576 | tf_op jit(solution)/shard_map/psum | solution.py:78
  551.7 3.0 copy-start.3
  551.7 3.0 copy-start.5
  551.7 3.0 copy-start.7
  556.2 1.4 copy-start.8
  556.2 1.4 copy-start.12
Sparse Core Ops, SparseCore 0:
  125.5 47.0 all-reduce.4
  252.0 46.2 all-reduce.6
  377.7 46.2 all-reduce.8
  505.4 46.2 all-reduce.10
where the time goes:
time: 566 us; the launch traced here: 565 us
  waiting for transfers between devices  277 us (49%)
  blocking collectives  164 us (29%)
  starting transfers between devices  46.2 us (8%)
  other arithmetic  30.4 us (5%)
  local copies, waits for them, and re-layouts  23.6 us (4%)
  between operations  14.9 us (3%)
  matrix products  9.37 us (2%)
    psum x4, waiting for transfers between devices, body(): lax.psum(partial_value.astype(jnp.bfloat16), 'blk').astype(jnp.float32)  171 us
    all_to_all x2, blocking collectives, body(): lax.all_to_all(outbound_rates, 'area', split_axis=0, concat_axis=0, tiled...  136 us
    all_to_all x2, waiting for transfers between devices, body(): lax.all_to_all(outbound_rates, 'area', split_axis=0, concat_axis=0, tiled...  106 us
    all_to_all x2, starting transfers between devices, body(): lax.all_to_all(outbound_rates, 'area', split_axis=0, concat_axis=0, tiled...  28.7 us
    all_to_all x1, starting transfers between devices, body(): lax.all_to_all(request_table, 'area', split_axis=0, concat_axis=0, tiled=...  17.4 us
    all_gather x1, blocking collectives, body(): lax.all_gather(ext_input.astype(jnp.float32).astype(jnp.bfloat16), 'blk',...  14.4 us
    all_gather x1, blocking collectives, body(): lax.all_gather(activity.astype(jnp.bfloat16), 'blk', axis=1, tiled=True)  13.1 us
  transfers between devices with their start and end apart: 7, of which 6 were waited for; matrix products, arithmetic and copies ran while one was open for 1% of the time, Pallas kernels for 0%

commit v1 on v0

--- a/solution.py
+++ b/solution.py
@@ -75,7 +75,9 @@
             "kd,kts->dts", select, input_contribution, precision=lax.Precision.HIGHEST
         )
         partial_value, presynaptic_rates = (partial_value, presynaptic_rates)
-        summed = lax.psum(partial_value.astype(jnp.bfloat16), "blk").astype(jnp.float32)
+        summed = jnp.sum(lax.all_gather(partial_value.astype(jnp.bfloat16), "blk"), axis=0).astype(
+            jnp.float32
+        )
         current = current + euler_step * (summed - current + drive_in)
         rate_full = jnp.tanh(current).astype(jnp.bfloat16)
         pre_list.append(presynaptic_rates)

time: 566 us -> 495 us (0.87)
  the two profiles are of different devices: /device:TPU:8 before, /device:TPU:1 now
where the time goes in v1:
time: 495 us; the launch traced here: 494 us
  blocking collectives  218 us (44%)
  waiting for transfers between devices  149 us (30%)
  other arithmetic  35.6 us (7%)
  starting transfers between devices  34.4 us (7%)
  local copies, waits for them, and re-layouts  31.6 us (6%)
  between operations  14.9 us (3%)
  matrix products  9.34 us (2%)
    all_to_all x3, blocking collectives, body(): lax.all_to_all(outbound_rates, 'area', split_axis=0, concat_axis=0, tiled...  197 us
    all_gather x4, waiting for transfers between devices, body(): lax.all_gather(partial_value.astype(jnp.bfloat16), 'blk')  98.6 us
    all_to_all x1, waiting for transfers between devices, body(): lax.all_to_all(outbound_rates, 'area', split_axis=0, concat_axis=0, tiled...  50.7 us
    all_to_all x1, starting transfers between devices, body(): lax.all_to_all(request_table, 'area', split_axis=0, concat_axis=0, tiled=...  18.4 us
    all_to_all x1, starting transfers between devices, body(): lax.all_to_all(outbound_rates, 'area', split_axis=0, concat_axis=0, tiled...  15.8 us
    all_gather x1, blocking collectives, body(): lax.all_gather(activity.astype(jnp.bfloat16), 'blk', axis=1, tiled=True)  11.7 us
    all_gather x1, blocking collectives, body(): lax.all_gather(ext_input.astype(jnp.float32).astype(jnp.bfloat16), 'blk',...  10 us
  transfers between devices with their start and end apart: 6, of which 5 were waited for; matrix products, arithmetic and copies ran while one was open for 4% of the time, Pallas kernels for 0%

profile of v1, /device:TPU:1, one launch (start us, length us, event | category | flops | bytes accessed | tf_op | source)
XLA Modules:
  0.0 493.7 jit_solution(9332497391056655408)
XLA Ops:
  9.6 18.4 %all-to-all-start = ((s32[128,1,1]{2,1,0:T(1,128)}), s32[128,1,1]{2,1,0:T(1,128)S(1)}, u32[]{:S(2)}, u32[]{:S(2)}) async-start(s32[128,1,1]{2,1,0:T(1,128)} %copy.68), calls=%async_computation | async-start | bytes 131072 | tf_op jit(solution)/shard_map/all_to_all | solution.py:43
  29.0 11.7 %all_gather.30 = bf16[8,4,64,128]{3,2,1,0:T(8,128)(2,1)S(1)} all-gather(bf16[8,1,64,128]{3,2,1,0:T(8,128)(2,1)S(1)} %convert_element_type.188), channel_id=1, replica_groups=mesh['area'=128,'blk'=4] {'blk'}, dimensions={1}, use_global_device_ids=true | all-gather | bytes 655360 | tf_op jit(solution)/shard_map/all_gather | solution.py:53
  42.1 2.4 maximum_reduce_fusion
  46.6 2.4 compare_reduce_fusion
  48.9 3.1 fusion.4
  52.1 15.8 %all-to-all-start.1 = ((bf16[128,1,64,128]{3,2,1,0:T(8,128)(2,1)}), bf16[128,1,64,128]{3,2,1,0:T(8,128)(2,1)}, u32[]{:S(2)}, u32[]{:S(2)}) async-start(bf16[128,1,64,128]{3,2,1,0:T(8,128)(2,1)} %fusion.4), calls=%async_computation.1 | async-start | bytes 4194304 | tf_op jit(solution)/shard_map/all_to_all | solution.py:68
  68.0 50.7 %all-to-all-done.1 = bf16[128,1,64,128]{3,2,1,0:T(8,128)(2,1)} async-done(((bf16[128,1,64,128]{3,2,1,0:T(8,128)(2,1)}), bf16[128,1,64,128]{3,2,1,0:T(8,128)(2,1)}, u32[]{:S(2)}, u32[]{:S(2)}) %all-to-all-start.1) | async-done | bytes 2097184 | tf_op jit(solution)/shard_map/all_to_all | solution.py:68
  118.8 2.2 gather_fusion.1
  123.0 10.0 %all_gather.33 = bf16[8,4,64,128]{3,2,1,0:T(8,128)(2,1)S(1)} all-gather(bf16[8,1,64,128]{3,2,1,0:T(8,128)(2,1)S(1)} %copy-done.19), channel_id=1, replica_groups=mesh['area'=128,'blk'=4] {'blk'}, dimensions={1}, use_global_device_ids=true | all-gather | bytes 655360 | tf_op jit(solution)/shard_map/all_gather | solution.py:56
  134.2 20.7 %all-gather.9.cloned.1.call-done = bf16[32,64,512]{2,0,1:T(8,128)(2,1)} async-done(((bf16[8,64,512]{2,0,1:T(8,128)(2,1)}), bf16[32,64,512]{2,0,1:T(8,128)(2,1)}) %all-gather.9.cloned.1.call-update) | async-done | bytes 2097168 | tf_op jit(solution)/shard_map/all_gather | solution.py:78
  157.8 2.2 gather_fusion.2
  161.8 65.6 %all_to_all.29 = bf16[128,1,64,128]{3,2,1,0:T(8,128)(2,1)} all-to-all(bf16[128,1,64,128]{3,2,1,0:T(8,128)(2,1)S(1)} %fusion.3), channel_id=1, replica_groups=mesh['area'=128,'blk'=4] {'area'}, dimensions={0} | all-to-all | bytes 4194304 | tf_op jit(solution)/shard_map/all_to_all | solution.py:68
  227.4 2.2 gather_fusion.3
  231.5 30.6 %all-gather.11.cloned.1.call-done = bf16[32,64,512]{2,0,1:T(8,128)(2,1)} async-done(((bf16[8,64,512]{2,0,1:T(8,128)(2,1)}), bf16[32,64,512]{2,0,1:T(8,128)(2,1)}) %all-gather.11.cloned.1.call-update) | async-done | bytes 2097168 | tf_op jit(solution)/shard_map/all_gather | solution.py:78
  266.2 2.2 gather_fusion.4
  270.2 65.5 %all_to_all.30 = bf16[128,1,64,128]{3,2,1,0:T(8,128)(2,1)S(1)} all-to-all(bf16[128,1,64,128]{3,2,1,0:T(8,128)(2,1)S(1)} %fusion.2), channel_id=1, replica_groups=mesh['area'=128,'blk'=4] {'area'}, dimensions={0} | all-to-all | bytes 4194304 | tf_op jit(solution)/shard_map/all_to_all | solution.py:68
  339.7 30.6 %all-gather.13.cloned.1.call-done = bf16[32,64,512]{2,0,1:T(8,128)(2,1)} async-done(((bf16[8,64,512]{2,0,1:T(8,128)(2,1)}), bf16[32,64,512]{2,0,1:T(8,128)(2,1)}) %all-gather.13.cloned.1.call-update) | async-done | bytes 2097168 | tf_op jit(solution)/shard_map/all_gather | solution.py:78
  373.7 2.2 gather_fusion.6
  377.7 65.6 %all_to_all.31 = bf16[128,1,64,128]{3,2,1,0:T(8,128)(2,1)} all-to-all(bf16[128,1,64,128]{3,2,1,0:T(8,128)(2,1)S(1)} %fusion.1), channel_id=1, replica_groups=mesh['area'=128,'blk'=4] {'area'}, dimensions={0} | all-to-all | bytes 4194304 | tf_op jit(solution)/shard_map/all_to_all | solution.py:68
  443.3 2.2 gather_fusion.7
  451.8 3.0 copy.67
  454.8 2.6 reshape.453
  457.5 3.1 tanh_convert_fusion.1
  461.4 16.7 %all-gather.15.cloned.1.call-done = bf16[32,64,512]{2,0,1:T(8,128)(2,1)} async-done(((bf16[8,64,512]{2,0,1:T(8,128)(2,1)}), bf16[32,64,512]{2,0,1:T(8,128)(2,1)}) %all-gather.15.cloned.1.call-update) | async-done | bytes 2097168 | tf_op jit(solution)/shard_map/all_gather | solution.py:78
  (110 shorter events, 47.3 us)
Async XLA Ops:
  7.2 113.8 %copy-start = (bf16[3,1,128,512]{3,2,1,0:T(8,128)(2,1)S(1)}, bf16[3,1,128,512]{3,2,1,0:T(8,128)(2,1)}, u32[]{:S(2)}) copy-start(bf16[3,1,128,512]{3,2,1,0:T(8,128)(2,1)} %param.9) | copy-start | bytes 1179652
  9.6 32.5 %all-to-all-start = ((s32[128,1,1]{2,1,0:T(1,128)}), s32[128,1,1]{2,1,0:T(1,128)S(1)}, u32[]{:S(2)}, u32[]{:S(2)}) async-start(s32[128,1,1]{2,1,0:T(1,128)} %copy.68), calls=%async_computation | async-start | bytes 131072 | tf_op jit(solution)/shard_map/all_to_all | solution.py:43
  52.1 15.9 %copy-start.20 = (s32[3]{0:T(128)S(1)}, s32[3]{0:T(128)}, u32[]{:S(2)}) copy-start(s32[3]{0:T(128)} %param.10) | copy-start | bytes 40
  52.1 66.7 %all-to-all-start.1 = ((bf16[128,1,64,128]{3,2,1,0:T(8,128)(2,1)}), bf16[128,1,64,128]{3,2,1,0:T(8,128)(2,1)}, u32[]{:S(2)}, u32[]{:S(2)}) async-start(bf16[128,1,64,128]{3,2,1,0:T(8,128)(2,1)} %fusion.4), calls=%async_computation.1 | async-start | bytes 4194304 | tf_op jit(solution)/shard_map/all_to_all | solution.py:68
  67.9 55.1 %copy-start.19 = (bf16[8,1,64,128]{3,2,1,0:T(8,128)(2,1)S(1)}, bf16[8,1,64,128]{3,2,1,0:T(8,128)(2,1)}, u32[]{:S(2)}) copy-start(bf16[8,1,64,128]{3,2,1,0:T(8,128)(2,1)} %param.8) | copy-start | bytes 393220
  67.9 87.0 %all-gather.9.cloned.1.call-start = ((), (), s32[]{:S(2)}) async-start(), calls=%async_computation.5 | async-start | bytes 2621440 | tf_op jit(solution)/shard_map/all_gather | solution.py:78
  121.0 2.0 copy-start.12
  122.9 139.2 %all-gather.11.cloned.1.call-start = ((), (), s32[]{:S(2)}) async-start(), calls=%async_computation.6 | async-start | bytes 2621440 | tf_op jit(solution)/shard_map/all_gather | solution.py:78
  229.5 1.9 copy-start.14
  231.4 138.9 %all-gather.13.cloned.1.call-start = ((), (), s32[]{:S(2)}) async-start(), calls=%async_computation.7 | async-start | bytes 2621440 | tf_op jit(solution)/shard_map/all_gather | solution.py:78
  337.9 34.4 %copy-start.2 = (f32[8,64,512]{2,1,0:T(8,128)S(1)}, f32[8,64,512]{2,1,0:T(8,128)}, u32[]{:S(2)}) copy-start(f32[8,64,512]{2,1,0:T(8,128)} %copy-done.1) | copy-start | bytes 3145732
  339.6 138.5 %all-gather.15.cloned.1.call-start = ((), (), s32[]{:S(2)}) async-start(), calls=%async_computation.8 | async-start | bytes 2621440 | tf_op jit(solution)/shard_map/all_gather | solution.py:78
  445.4 3.0 copy-start.17
  445.5 3.0 copy-start.8
  451.8 5.6 %copy-start.21 = (s32[3]{0:T(128)S(1)}, s32[3]{0:T(128)}, u32[]{:S(2)}) copy-start(s32[3]{0:T(128)} %param.10) | copy-start | bytes 40
  451.8 5.6 %copy-start.22 = (s32[3]{0:T(128)S(1)}, s32[3]{0:T(128)}, u32[]{:S(2)}) copy-start(s32[3]{0:T(128)} %param.13) | copy-start | bytes 40
  451.8 5.7 %copy-start.4 = (bf16[8,64,512]{2,0,1:T(8,128)(2,1)S(1)}, bf16[8,64,512]{2,0,1:T(8,128)(2,1)}, u32[]{:S(2)}) copy-start(bf16[8,64,512]{2,0,1:T(8,128)(2,1)} %copy-done.3) | copy-start | bytes 1572868
  451.8 5.7 %copy-start.6 = (bf16[8,64,512]{2,0,1:T(8,128)(2,1)S(1)}, bf16[8,64,512]{2,0,1:T(8,128)(2,1)}, u32[]{:S(2)}) copy-start(bf16[8,64,512]{2,0,1:T(8,128)(2,1)} %copy-done.5) | copy-start | bytes 1572868
  457.5 3.1 copy-start.13
  457.5 3.1 copy-start.15
  457.5 3.1 copy-start.16
  457.5 3.1 copy-start.18
  478.2 3.3 copy-start.9
  483.6 2.5 copy-start.11
  (5 other events, 4.6 us)
Sparse Core Ops, SparseCore 0:
  123.0 31.8 all-gather.8
  231.6 30.5 all-gather.10
  339.8 30.5 all-gather.12
  447.5 30.6 all-gather.14
